TPU v7x, 32 devices: a whole 2x2x4 slice. The times are simulated.
32 devices in a mesh: dp: 2 (over core), expert: 16 (over z, y, x).
Axes of the slice: x: 2, y: 2, z: 4, core: 2. Of those that a mesh axis runs over, the one named last changes fastest.
Arguments:
- grad_out: bfloat16 [4096, 2048], P(('dp', 'expert')), may hold values from -0.59765625 to 0.59765625
- routes: int32 [4096, 8], P(('dp', 'expert')), may hold values from 0 to 15, all different within a row; in each aligned block of 128 rows (0 to 127, 128 to 255, ...) at most 96 rows name the same one
- router_probs: float32 [4096, 8], P(('dp', 'expert')), may hold values from 0.02 to 1
- saved_hidden: bfloat16 [16, 2, 1536, 768], P('expert', 'dp'), may hold values from -1.796875 to 1.796875
- down_weight: bfloat16 [16, 768, 2048], P('expert', 'dp'), may hold values from -0.21875 to 0.21875
- moment_one: bfloat16 [16, 768, 2048], P('expert', 'dp'), may hold values from -0.59765625 to 0.59765625
- moment_two: bfloat16 [16, 768, 2048], P('expert', 'dp'), may hold values from 0.0099487305 to 0.5
- partner: int32 [16], replicated, may hold values from 0 to 15, as said below
Outputs:
- gate_grad: float32 [4096, 8], P(('dp', 'expert'))
- new_down: bfloat16 [16, 768, 2048], P('expert', 'dp')
- new_moment_one: bfloat16 [16, 768, 2048], P('expert', 'dp')
- new_moment_two: bfloat16 [16, 768, 2048], P('expert', 'dp')
Inputs may be any that keep to these rules, and one draw needn't show every extreme that they name: `routes`: each row names 8 different experts. Among the 128 rows of one device no expert is named more than 96 times, and on some device an expert is named exactly 96 times. partner[partner[i]] = i, and partner[i] is either i or differs from i in exactly one bit.
All inputs are finite; a program needn't handle non-finite values.
Results may differ from a plain program's by a relative error of at most 0.0055.
Values may be sent and summed in bfloat16 or wider, within the bound.
No kernel may reach another device: no remote copies, remote signals or barrier semaphores. Data moves between devices by JAX's collectives and lax.ppermute only.
A program may use at most 128 MiB of HBM per device.

v0:
```python
import jax
import jax.numpy as jnp
from jax import lax
from jax.sharding import PartitionSpec as P
from jax.experimental.layout import Layout, with_layout_constraint

beta_one = 0.9
beta_two = 0.95
learn_rate = 0.001
weight_decay = 0.1
adam_epsilon = 1e-08
step_count = 1000

gather_limit_bytes = 16 * 1024 * 1024


def adam_update(weight, moment_first, moment_second, grad_sum):
    first_new = beta_one * moment_first.astype(jnp.float32) + (1.0 - beta_one) * grad_sum
    second_new = (
        beta_two * moment_second.astype(jnp.float32) + (1.0 - beta_two) * grad_sum * grad_sum
    )
    corr_one = 1.0 - beta_one**step_count
    corr_two = 1.0 - beta_two**step_count
    weight_full = weight.astype(jnp.float32)
    direction = first_new / corr_one / (jnp.sqrt(second_new / corr_two) + adam_epsilon)
    updated = weight_full - learn_rate * (direction + weight_decay * weight_full)
    return (
        updated.astype(jnp.bfloat16),
        first_new.astype(jnp.bfloat16),
        second_new.astype(jnp.bfloat16),
    )


def block_ranks(hit):
    return jnp.cumsum(hit.astype(jnp.int32), axis=-1) - 1


def slot_onehot(hit, rank, capacity):
    slot_iota = jnp.arange(capacity, dtype=jnp.int32)
    return hit[..., None, :] & (rank[..., None, :] == slot_iota[:, None])


def on_device(
    grad_out, routes, router_probs, saved_hidden, down_weight, moment_one, moment_two, partner
):
    tok_rows, top_count = routes.shape
    width = grad_out.shape[1]
    axis_size = lax.axis_size("expert")
    me = lax.axis_index("expert")
    expert_count = partner.shape[0]
    capacity = 3 * tok_rows * top_count // (2 * expert_count)
    slot_count = capacity * axis_size

    weight = down_weight[0]
    weight_full = lax.all_gather(weight, "dp", axis=0, tiled=True)
    hidden = saved_hidden[0, 0]

    prob_sum = jnp.sum(router_probs, axis=1, keepdims=True)
    gate_share = router_probs / prob_sum
    gate_low = gate_share.astype(jnp.bfloat16)

    expert_iota = jnp.arange(expert_count, dtype=jnp.int32)
    local_hit = jnp.any(routes[:, :, None] == expert_iota[None, None, :], axis=1)
    local_rank = block_ranks(local_hit.T).T
    pair_rank = jnp.take_along_axis(local_rank, routes, axis=1)

    mine = partner[me]
    levels = axis_size.bit_length() - 1
    device_iota = jnp.arange(expert_count, dtype=jnp.int32)
    which = jnp.int32(0)
    for level in range(levels):
        which = which + jnp.where(mine == (me ^ (1 << level)), level + 1, 0).astype(jnp.int32)

    optional = list(range(max(levels - 2, 0), levels))
    fixed = list(range(levels - len(optional)))
    units = []
    choice = jnp.int32(0)
    member_of = []
    if optional:
        units += [(level, list(range(axis_size))) for level in optional[:-1]]
        top = optional[-1]
        other = optional[0] if len(optional) > 1 else None
        for value in range(2 if other is not None else 1):
            members = [i for i in range(axis_size) if other is None or (i >> other & 1) == value]
            units.append((top, members))
        for position, (level, members) in enumerate(units):
            member_iota = jnp.asarray(members, dtype=jnp.int32)
            used = jnp.any(partner[member_iota] == (member_iota ^ (1 << level)))
            choice = choice + jnp.where(used, 1 << position, 0).astype(jnp.int32)
            member_of.append(jnp.any(member_iota == me))


    gather_bytes = axis_size * tok_rows * width * grad_out.dtype.itemsize
    if gather_bytes <= gather_limit_bytes:
        packed = jnp.concatenate([routes.astype(jnp.float32), router_probs], axis=1)
        hidden_t, packed = lax.optimization_barrier((hidden.T, packed))
        packed_all = lax.all_gather(packed, "expert", axis=0, tiled=True)
        grad_all = lax.all_gather(grad_out, "expert", axis=0, tiled=True)
        routes_all = packed_all[:, :top_count].astype(jnp.int32)
        probs_all = packed_all[:, top_count:]
        gate_all = (probs_all / jnp.sum(probs_all, axis=1, keepdims=True)).astype(jnp.bfloat16)
        hit_k = routes_all == me
        hit = jnp.any(hit_k, axis=1).reshape(axis_size, tok_rows)
        gate_tok = jnp.sum(
            jnp.where(hit_k, gate_all.astype(jnp.float32), 0.0), axis=1
        ).reshape(axis_size, tok_rows)
        onehot = slot_onehot(hit, block_ranks(hit), capacity)
        dispatched = jnp.einsum(
            "sjt,std->sjd",
            onehot.astype(jnp.bfloat16),
            grad_all.reshape(axis_size, tok_rows, width),
            preferred_element_type=jnp.float32,
        ).astype(jnp.bfloat16)
        slot_gate = jnp.sum(
            jnp.where(onehot, gate_tok[:, None, :], 0.0), axis=2
        ).astype(jnp.bfloat16)
    else:
        hidden_t = hidden.T
        gate_pair = jnp.sum(
            jnp.where(
                routes[:, :, None] == expert_iota[None, None, :],
                gate_low.astype(jnp.float32)[:, :, None],
                0.0,
            ),
            axis=1,
        )
        onehot = slot_onehot(local_hit.T, local_rank.T, capacity)
        send_rows = jnp.einsum(
            "ejt,td->ejd",
            onehot.astype(jnp.bfloat16),
            grad_out,
            preferred_element_type=jnp.float32,
        ).astype(jnp.bfloat16)
        send_gate = jnp.sum(jnp.where(onehot, gate_pair.T[:, None, :], 0.0), axis=2).astype(
            jnp.bfloat16
        )
        dispatched = lax.all_to_all(send_rows, "expert", split_axis=0, concat_axis=0, tiled=True)
        slot_gate = lax.all_to_all(send_gate, "expert", split_axis=0, concat_axis=0, tiled=True)

    dispatched = dispatched.reshape(slot_count, width)
    dispatched, which, choice, member_of = lax.optimization_barrier(
        (dispatched, which, choice, member_of)
    )
    slot_gate = slot_gate.reshape(slot_count)
    scaled = slot_gate[:, None] * dispatched
    projected = lax.dot_general(
        dispatched,
        weight_full,
        (((1,), (1,)), ((), ())),
        preferred_element_type=jnp.float32,
    )
    products = jnp.sum(hidden.astype(jnp.float32) * projected, axis=1)
    grad_full = lax.dot_general(
        hidden_t, scaled, (((1,), (0,)), ((), ())), preferred_element_type=jnp.float32
    ).astype(jnp.bfloat16)
    grad_full = with_layout_constraint(grad_full, Layout(major_to_minor=(0, 1)))
    grad_sum = lax.psum_scatter(
        grad_full,
        "dp",
        scatter_dimension=0,
        tiled=True,
    ).astype(jnp.float32)
    returned = lax.all_to_all(
        products.reshape(axis_size, capacity), "expert", split_axis=0, concat_axis=0, tiled=True
    )
    expert_rows = jnp.sum(
        jnp.where(
            (routes[:, :, None] == expert_iota)[..., None], returned[None, None, :, :], 0.0
        ),
        axis=2,
    )
    answer = jnp.sum(
        jnp.where(pair_rank[..., None] == jnp.arange(capacity), expert_rows, 0.0), axis=2
    )
    gate_grad = (answer - jnp.sum(gate_share * answer, axis=1, keepdims=True)) / prob_sum

    outputs = jnp.stack(adam_update(weight, moment_one[0], moment_two[0], grad_sum))
    outputs = with_layout_constraint(outputs, Layout(major_to_minor=(0, 1, 2)))
    outputs, gate_grad = lax.optimization_barrier((outputs, gate_grad))

    def exchange(arrays, level, pairs=None):
        flip = 1 << level
        pairs = range(axis_size) if pairs is None else pairs
        return lax.ppermute(arrays, "expert", perm=[(i, i ^ flip) for i in pairs])

    cases = [outputs] + [exchange(outputs, level) for level in fixed]
    if optional:
        def branch(mask):
            def run(arrays):
                picks = [arrays]
                index = jnp.int32(0)
                for position, (level, members) in enumerate(units):
                    if mask >> position & 1:
                        picks.append(exchange(arrays, level, members))
                        hit = (which == level + 1) & member_of[position]
                        index = index + jnp.where(hit, len(picks) - 1, 0).astype(jnp.int32)
                return lax.select_n(index, *picks) if len(picks) > 1 else arrays

            return run

        cases[0] = lax.switch(choice, [branch(mask) for mask in range(1 << len(units))], outputs)
    top_index = jnp.where(which <= len(fixed), which, 0)
    landed = lax.select_n(top_index, *cases)
    return (gate_grad, landed[0][None], landed[1][None], landed[2][None])


def solution(mesh):
    in_specs = (
        P(("dp", "expert"), None),
        P(("dp", "expert"), None),
        P(("dp", "expert"), None),
        P("expert", "dp", None, None),
        P("expert", "dp", None),
        P("expert", "dp", None),
        P("expert", "dp", None),
        P(),
    )
    out_specs = (
        P(("dp", "expert"), None),
        P("expert", "dp", None),
        P("expert", "dp", None),
        P("expert", "dp", None),
    )
    return jax.shard_map(
        on_device, mesh=mesh, in_specs=in_specs, out_specs=out_specs, check_vma=False
    )
```

profile of v0, /device:TPU:8, one launch (start us, length us, event | category | flops | bytes accessed | tf_op | source)
XLA Modules:
  0.0 292.9 jit_solution(5048564278247043432)
XLA Ops:
  7.2 0.7 all-gather.4.cloned.1.call-update
  7.9 0.7 all-gather.6.cloned.1.call-update
  8.7 0.7 fusion.22
  9.4 0.7 bitcast_or_fusion
  10.1 2.8 copy.39
  13.5 7.0 %gather_fusion.3 = s32[1024]{0:T(1024)S(1)} fusion(s32[128,16]{0,1:T(8,128)S(1)} %add_bitcast_fusion, s32[1024]{0:T(1024)S(1)} %reshape.91), kind=kCustom, calls=%fused_computation.3 | custom fusion | bytes 16384 | tf_op jit(solution)/shard_map/jit(take_along_axis)/gather | solution.py:65
  20.7 36.1 %all_gather.9 = f32[2048,16]{0,1:T(8,128)S(1)} all-gather(f32[128,16]{0,1:T(8,128)S(1)} %pad_maximum_fusion.1), channel_id=1, replica_groups=mesh['dp'=2,'expert'=16] {'expert'}, dimensions={0}, use_global_device_ids=true | all-gather | bytes 139264 | tf_op jit(solution)/shard_map/all_gather | solution.py:97
  56.9 0.6 compare_reduce_fusion.2
  61.1 0.7 gather_fusion
  61.7 0.6 compare_reduce_fusion.5
  63.1 0.6 gather_fusion.1
  63.7 0.6 compare_reduce_fusion.4
  65.0 0.6 gather_fusion.2
  65.7 0.6 compare_reduce_fusion.3
  67.5 0.7 compare_reduce_fusion
  68.1 56.7 %all-gather.4.cloned.1.call-done = bf16[2048,2048]{1,0:T(8,128)(2,1)} async-done(((bf16[128,2048]{1,0:T(8,128)(2,1)}), bf16[2048,2048]{1,0:T(8,128)(2,1)}) %all-gather.4.cloned.1.call-update) | async-done | bytes 8388624 | tf_op jit(solution)/shard_map/all_gather | solution.py:98
  124.8 5.2 %convolution_convert_fusion = bf16[16,96,2048]{2,1,0:T(8,128)(2,1)S(1)} fusion(bf16[16,128,2048]{2,1,0:T(8,128)(2,1)} %bitcast.56, s32[16,128]{1,0:T(8,128)S(1)} %broadcast_add_fusion, pred[16,128]{1,0:T(8,128)(4,1)S(1)} %bitcast.61), kind=kOutput, calls=%fused_computation.18 | convolution fusion | flops 808845312 | bytes 14690304 | tf_op jit(solution)/shard_map/sjt,std->sjd/dot_general | solution.py:108
  130.0 2.6 copy-done.1
  132.6 6.6 %fusion.2 = bf16[768,2048]{1,0:T(8,128)(2,1)} fusion(bf16[768,1536]{1,0:T(8,128)(2,1)S(1)} %bitcast.59, bf16[1536,2048]{1,0:T(8,128)(2,1)S(1)} %bitcast.57, bf16[1536]{0:T(1024)(128)(2,1)S(1)} %convert_element_type.76), kind=kOutput, calls=%fused_computation.22 | convolution fusion | flops 4836556800 | bytes 11799552 | tf_op jit(solution)/shard_map/dot_general | solution.py:153
  139.3 8.7 %multiply_reduce_fusion = f32[1536]{0:T(1024)S(1)} fusion(bf16[1536,2048]{1,0:T(8,128)(2,1)} %bitcast.58, bf16[1,768,2048]{2,1,0:T(8,128)(2,1)} %all-gather.6.cloned.1.call-done, bf16[1,1,1536,768]{2,3,1,0:T(8,128)(2,1)} %copy-done.3), kind=kOutput, calls=%fused_computation.17 | convolution fusion | flops 4835375616 | bytes 11802624 | tf_op jit(solution)/shard_map/dot_general | solution.py:146
  148.0 0.7 all_to_all.6
  148.6 5.9 %all-to-all-start = ((f32[16,1,96]{2,1,0:T(1,128)}), f32[16,1,96]{2,1,0:T(1,128)S(1)}, u32[]{:S(2)}, u32[]{:S(2)}) async-start(f32[16,1,96]{2,1,0:T(1,128)} %all_to_all.6), calls=%async_computation.1 | async-start | bytes 16384 | tf_op jit(solution)/shard_map/all_to_all | solution.py:163
  154.6 5.8 %all-to-all-done = f32[16,1,96]{2,1,0:T(1,128)S(1)} async-done(((f32[16,1,96]{2,1,0:T(1,128)}), f32[16,1,96]{2,1,0:T(1,128)S(1)}, u32[]{:S(2)}, u32[]{:S(2)}) %all-to-all-start) | async-done | bytes 6176 | tf_op jit(solution)/shard_map/all_to_all | solution.py:163
  160.4 0.8 select_reduce_fusion
  161.9 4.1 %fusion.16 = (bf16[1,384,2048]{2,1,0:T(8,128)(2,1)S(1)}, bf16[1,384,2048]{2,1,0:T(8,128)(2,1)S(1)}, bf16[1,384,2048]{2,1,0:T(8,128)(2,1)S(1)}) fusion(bf16[1,384,2048]{2,1,0:T(8,128)(2,1)S(1)} %copy-done.4, bf16[384,2048]{1,0:T(8,128)(2,1)} %reduce-scatter.2.cloned.1.call-done, bf16[1,384,2048]{2,1,0:T(8,128)(2,1)} %param.24, ...), kind=kLoop, calls=%fused_computation.34 | loop fusion | flops 15728640 | bytes 11010048 | tf_op jit(solution)/shard_map/stack | solution.py:177
  166.1 2.4 pad_maximum_fusion
  169.6 110.0 %conditional.1 = (bf16[3,384,2048]{2,1,0:T(8,128)(2,1)}) conditional(s32[]{:T(128)} %clamp.3, bf16[3,384,2048]{2,1,0:T(8,128)(2,1)} %pad_maximum_fusion, (s32[]{:T(128)}, pred[]{:T(512)}, bf16[3,384,2048]{2,1,0:T(8,128)(2,1)}) %tuple.38, (s32[]{:T(128)}, pred[]{:T(512)}, bf16[3,384,2048]{2,1,0:T(8,128)(2,1)}) %tuple.39, ...), branch_computations={%region_19.20_spmd, %region_20.21_spmd, %region_21.22_spmd, %regio... | conditional | flops 7077901 | bytes 80216312 | solution.py:201
  169.6 2.5 collective-permute-start.4
  172.7 101.9 %collective-permute-done.4 = bf16[3,384,2048]{2,1,0:T(8,128)(2,1)} collective-permute-done((bf16[3,384,2048]{2,1,0:T(8,128)(2,1)}, bf16[3,384,2048]{2,1,0:T(8,128)(2,1)}, u32[]{:S(2)}, u32[]{:S(2)}) %collective-permute-start.4) | collective-permute-done | bytes 4718624 | tf_op jit(solution)/shard_map/cond/branch_4_fun/ppermute | solution.py:184
  274.6 5.0 %broadcast_select_fusion.2 = bf16[3,384,2048]{2,1,0:T(8,128)(2,1)} fusion(bf16[3,384,2048]{2,1,0:T(8,128)(2,1)} %get-tuple-element.74, bf16[3,384,2048]{2,1,0:T(8,128)(2,1)} %collective-permute-done.4, pred[]{:T(512)S(6)} %select_n.171), kind=kLoop, calls=%fused_computation.7 | loop fusion | flops 2359296 | bytes 14155777 | tf_op jit(solution)/shard_map/cond/branch_4_fun/select_n | solution.py:197
  279.6 4.4 %select_select_fusion.4 = bf16[3,384,2048]{2,1,0:T(8,128)(2,1)S(1)} fusion(bf16[3,384,2048]{2,1,0:T(8,128)(2,1)} %get-tuple-element.126, bf16[3,384,2048]{2,1,0:T(8,128)(2,1)} %collective-permute-done.12, bf16[3,384,2048]{2,1,0:T(8,128)(2,1)} %collective-permute-done.13, pred[]{:T(512)S(6)} %select_n.246, pred[]{:T(512)S(6)} %select_n.244), kind=kLoop, calls=%fused_computation.16 | loop fusion | flops 4718592 | bytes 18874370 | tf_op jit(solution)/shard_map/select_n | solution.py:203
  284.0 2.4 fusion.24
  (57 shorter events, 4.2 us)
Async XLA Ops:
  7.2 117.7 %all-gather.4.cloned.1.call-start = ((), (), s32[]{:S(2)}) async-start(), calls=%async_computation.2 | async-start | bytes 8912896 | tf_op jit(solution)/shard_map/all_gather | solution.py:98
  7.9 131.4 %all-gather.6.cloned.1.call-start = ((), (), s32[]{:S(2)}) async-start(), calls=%async_computation.4 | async-start | bytes 4718592 | tf_op jit(solution)/shard_map/all_gather | solution.py:55
  8.6 153.3 %reduce-scatter.2.cloned.1.call-start = ((), (), s32[]{:S(2)}) async-start(), calls=%async_computation.3 | async-start | bytes 4718592 | tf_op jit(solution)/shard_map/reduce_scatter | solution.py:157
  12.9 117.1 %copy-start.3 = (bf16[1,1,1536,768]{2,3,1,0:T(8,128)(2,1)}, bf16[1,1,1536,768]{2,3,1,0:T(8,128)(2,1)S(1)}, u32[]{:S(2)}) copy-start(bf16[1,1,1536,768]{2,3,1,0:T(8,128)(2,1)S(1)} %copy.39) | copy-start | bytes 7077892
  13.4 7.3 %copy-start.6 = (s32[128,8]{0,1:T(8,128)S(1)}, s32[128,8]{0,1:T(8,128)}, u32[]{:S(2)}) copy-start(s32[128,8]{0,1:T(8,128)} %param.20) | copy-start | bytes 12292
  13.5 7.3 %copy-start.5 = (f32[128,8]{0,1:T(8,128)S(1)}, f32[128,8]{0,1:T(8,128)}, u32[]{:S(2)}) copy-start(f32[128,8]{0,1:T(8,128)} %param.21) | copy-start | bytes 12292
  13.5 44.4 %copy-start = (s32[16]{0:T(128)S(1)}, s32[16]{0:T(128)}, u32[]{:S(2)}) copy-start(s32[16]{0:T(128)} %param.26) | copy-start | bytes 196
  13.5 49.6 %copy-start.7 = (s32[8]{0:T(128)S(1)}, s32[8]{0:T(128)}, u32[]{:S(2)}) copy-start(s32[8]{0:T(128)} %constant.72.clone) | copy-start | bytes 100
  13.5 50.2 %copy-start.10 = (s32[8]{0:T(128)S(1)}, s32[8]{0:T(128)}, u32[]{:S(2)}) copy-start(s32[8]{0:T(128)} %constant.138) | copy-start | bytes 100
  13.5 51.5 %copy-start.8 = (s32[8]{0:T(128)S(1)}, s32[8]{0:T(128)}, u32[]{:S(2)}) copy-start(s32[8]{0:T(128)} %constant.128.clone) | copy-start | bytes 100
  13.5 52.2 %copy-start.9 = (s32[8]{0:T(128)S(1)}, s32[8]{0:T(128)}, u32[]{:S(2)}) copy-start(s32[8]{0:T(128)} %constant.143) | copy-start | bytes 100
  130.0 2.7 copy-start.1
  139.2 22.7 %copy-start.2 = (bf16[1,384,2048]{2,1,0:T(8,128)(2,1)S(1)}, bf16[1,384,2048]{2,1,0:T(8,128)(2,1)}, u32[]{:S(2)}) copy-start(bf16[1,384,2048]{2,1,0:T(8,128)(2,1)} %param.23) | copy-start | bytes 4718596
  139.2 22.7 %copy-start.4 = (bf16[1,384,2048]{2,1,0:T(8,128)(2,1)S(1)}, bf16[1,384,2048]{2,1,0:T(8,128)(2,1)}, u32[]{:S(2)}) copy-start(bf16[1,384,2048]{2,1,0:T(8,128)(2,1)} %param.25) | copy-start | bytes 4718596
  148.6 11.8 %all-to-all-start = ((f32[16,1,96]{2,1,0:T(1,128)}), f32[16,1,96]{2,1,0:T(1,128)S(1)}, u32[]{:S(2)}, u32[]{:S(2)}) async-start(f32[16,1,96]{2,1,0:T(1,128)} %all_to_all.6), calls=%async_computation.1 | async-start | bytes 16384 | tf_op jit(solution)/shard_map/all_to_all | solution.py:163
  168.5 111.1 %collective-permute-start.12 = (bf16[3,384,2048]{2,1,0:T(8,128)(2,1)}, bf16[3,384,2048]{2,1,0:T(8,128)(2,1)}, u32[]{:S(2)}, u32[]{:S(2)}) collective-permute-start(bf16[3,384,2048]{2,1,0:T(8,128)(2,1)} %pad_maximum_fusion), channel_id=1, source_target_pairs={{0,1},{1,0},{2,3},{3,2},{4,5},{5,4},{6,7},{7,6},{8,9},{9,8},{10,11... | collective-permute-start | bytes 14155784 | tf_op jit(solution)/shard_map/ppermute | solution.py:184
  169.0 110.5 %collective-permute-start.13 = (bf16[3,384,2048]{2,1,0:T(8,128)(2,1)}, bf16[3,384,2048]{2,1,0:T(8,128)(2,1)}, u32[]{:S(2)}, u32[]{:S(2)}) collective-permute-start(bf16[3,384,2048]{2,1,0:T(8,128)(2,1)} %pad_maximum_fusion), channel_id=1, source_target_pairs={{0,2},{1,3},{2,0},{3,1},{4,6},{5,7},{6,4},{7,5},{8,10},{9,11},{10,... | collective-permute-start | bytes 14155784 | tf_op jit(solution)/shard_map/ppermute | solution.py:184
  169.6 105.0 %collective-permute-start.4 = (bf16[3,384,2048]{2,1,0:T(8,128)(2,1)}, bf16[3,384,2048]{2,1,0:T(8,128)(2,1)}, u32[]{:S(2)}, u32[]{:S(2)}) collective-permute-start(bf16[3,384,2048]{2,1,0:T(8,128)(2,1)} %get-tuple-element.74), channel_id=1, source_target_pairs={{4,12},{5,13},{6,14},{7,15},{12,4},{13,5},{14,6},{15,7},{20,28},{2... | collective-permute-start | bytes 14155784 | tf_op jit(solution)/shard_map/cond/branch_4_fun/ppermute | solution.py:184
Sparse Core Ops, SparseCore 0:
  10.8 113.9 all-gather.3
  126.4 11.7 all-gather.5
  140.4 12.0 reduce-scatter.1
where the time goes:
time: 291 us; the launch traced here: 293 us
  waiting for transfers between devices  166 us (57%)
  blocking collectives  36.1 us (12%)
  other arithmetic  23.1 us (8%)
  matrix products  20.4 us (7%)
  local copies, waits for them, and re-layouts  18.6 us (6%)
  between operations  18.6 us (6%)
  starting transfers between devices  9.67 us (3%)
    ppermute x3, waiting for transfers between devices, exchange(): return lax.ppermute(arrays, 'expert', perm=[(i, i ^ flip) for i in pairs])  102 us
    all_gather x1, waiting for transfers between devices, on_device(): grad_all = lax.all_gather(grad_out, 'expert', axis=0, tiled=True)  56.7 us
    all_gather x1, blocking collectives, on_device(): packed_all = lax.all_gather(packed, 'expert', axis=0, tiled=True)  36.1 us
    dot_general x1, matrix products, on_device(): lax.dot_general(dispatched, weight_full, (((1,), (1,)), ((), ())), prefer...  8.68 us
    gather x5, local copies, waits for them, and re-layouts, on_device(): pair_rank = jnp.take_along_axis(local_rank, routes, axis=1)  7.34 us
    dot_general x1, matrix products, on_device(): lax.dot_general(hidden_t, scaled, (((1,), (0,)), ((), ())), preferred_ele...  6.56 us
    another operation x2, other arithmetic, on_device(): jnp.stack(adam_update(weight, moment_one[0], moment_two[0], grad_sum))  6.55 us
    all_to_all x1, starting transfers between devices, on_device(): lax.all_to_all(products.reshape(axis_size, capacity), 'expert', split_axi...  5.93 us
  transfers between devices with their start and end apart: 7, of which 3 were waited for; matrix products, arithmetic and copies ran while one was open for 15% of the time, Pallas kernels for 0%

commit v1 on v0

--- a/solution.py
+++ b/solution.py
@@ -160,9 +160,12 @@
         scatter_dimension=0,
         tiled=True,
     ).astype(jnp.float32)
+    outputs = jnp.stack(adam_update(weight, moment_one[0], moment_two[0], grad_sum))
+    outputs = with_layout_constraint(outputs, Layout(major_to_minor=(0, 1, 2)))
     returned = lax.all_to_all(
         products.reshape(axis_size, capacity), "expert", split_axis=0, concat_axis=0, tiled=True
     )
+    outputs, returned = lax.optimization_barrier((outputs, returned))
     expert_rows = jnp.sum(
         jnp.where(
             (routes[:, :, None] == expert_iota)[..., None], returned[None, None, :, :], 0.0
@@ -174,9 +177,6 @@
     )
     gate_grad = (answer - jnp.sum(gate_share * answer, axis=1, keepdims=True)) / prob_sum
 
-    outputs = jnp.stack(adam_update(weight, moment_one[0], moment_two[0], grad_sum))
-    outputs = with_layout_constraint(outputs, Layout(major_to_minor=(0, 1, 2)))
-    outputs, gate_grad = lax.optimization_barrier((outputs, gate_grad))
 
     def exchange(arrays, level, pairs=None):
         flip = 1 << level

time: 291 us -> 390 us (1.34)
  waiting for transfers between devices: 166 us -> 257 us
  starting transfers between devices: 9.67 us -> 13.9 us
    ppermute x3 -> x4, waiting for transfers between devices: 102 us -> 199 us  [exchange(): return lax.ppermute(arrays, 'expert', perm=[(i, i ^ flip) for i in pairs])]
    all_to_all x1, waiting for transfers between devices: 5.83 us -> 0.01 us  [on_device(): lax.all_to_all(products.reshape(axis_size, capacity), 'expert', split_axi...]
    ppermute x3 -> x4, starting transfers between devices: 3.63 us -> 7.82 us  [exchange(): return lax.ppermute(arrays, 'expert', perm=[(i, i ^ flip) for i in pairs])]
  transfers between devices with their start and end apart: 7 -> 8, of which waited for: 3 -> 3; matrix products, arithmetic and copies ran while one was open for 15% -> 13% of each run, Pallas kernels for 0% -> 0%
where the time goes in v1:
time: 390 us; the launch traced here: 389 us
  waiting for transfers between devices  257 us (66%)
  blocking collectives  36.1 us (9%)
  other arithmetic  23.3 us (6%)
  matrix products  20.4 us (5%)
  local copies, waits for them, and re-layouts  18.6 us (5%)
  between operations  18.6 us (5%)
  starting transfers between devices  13.9 us (4%)
    ppermute x4, waiting for transfers between devices, exchange(): return lax.ppermute(arrays, 'expert', perm=[(i, i ^ flip) for i in pairs])  199 us
    all_gather x1, waiting for transfers between devices, on_device(): grad_all = lax.all_gather(grad_out, 'expert', axis=0, tiled=True)  56.7 us
    all_gather x1, blocking collectives, on_device(): packed_all = lax.all_gather(packed, 'expert', axis=0, tiled=True)  36.1 us
    dot_general x1, matrix products, on_device(): lax.dot_general(dispatched, weight_full, (((1,), (1,)), ((), ())), prefer...  8.68 us
    ppermute x4, starting transfers between devices, exchange(): return lax.ppermute(arrays, 'expert', perm=[(i, i ^ flip) for i in pairs])  7.82 us
  transfers between devices with their start and end apart: 8, of which 3 were waited for; matrix products, arithmetic and copies ran while one was open for 13% of the time, Pallas kernels for 0%

profile of v1, /device:TPU:8, one launch (start us, length us, event | category | flops | bytes accessed | tf_op | source)
XLA Modules:
  0.0 389.2 jit_solution(3717648130418041056)
XLA Ops:
  7.2 0.7 all-gather.4.cloned.1.call-update
  7.9 0.7 all-gather.6.cloned.1.call-update
  8.7 0.7 fusion.22
  9.4 0.7 bitcast_or_fusion
  10.1 2.8 copy.41
  13.5 7.0 %gather_fusion.3 = s32[1024]{0:T(1024)S(1)} fusion(s32[128,16]{0,1:T(8,128)S(1)} %add_bitcast_fusion, s32[1024]{0:T(1024)S(1)} %reshape.90), kind=kCustom, calls=%fused_computation.3 | custom fusion | bytes 16384 | tf_op jit(solution)/shard_map/jit(take_along_axis)/gather | solution.py:65
  20.7 36.1 %all_gather.9 = f32[2048,16]{0,1:T(8,128)S(1)} all-gather(f32[128,16]{0,1:T(8,128)S(1)} %pad_maximum_fusion.1), channel_id=1, replica_groups=mesh['dp'=2,'expert'=16] {'expert'}, dimensions={0}, use_global_device_ids=true | all-gather | bytes 139264 | tf_op jit(solution)/shard_map/all_gather | solution.py:97
  61.1 0.7 gather_fusion
  61.7 0.6 compare_reduce_fusion.5
  63.1 0.6 gather_fusion.1
  63.7 0.6 compare_reduce_fusion.4
  65.0 0.6 gather_fusion.2
  67.5 0.7 compare_reduce_fusion
  68.1 56.7 %all-gather.4.cloned.1.call-done = bf16[2048,2048]{1,0:T(8,128)(2,1)} async-done(((bf16[128,2048]{1,0:T(8,128)(2,1)}), bf16[2048,2048]{1,0:T(8,128)(2,1)}) %all-gather.4.cloned.1.call-update) | async-done | bytes 8388624 | tf_op jit(solution)/shard_map/all_gather | solution.py:98
  124.8 5.2 %convolution_convert_fusion = bf16[16,96,2048]{2,1,0:T(8,128)(2,1)S(1)} fusion(bf16[16,128,2048]{2,1,0:T(8,128)(2,1)} %bitcast.56, s32[16,128]{1,0:T(8,128)S(1)} %broadcast_add_fusion, pred[16,128]{1,0:T(8,128)(4,1)S(1)} %bitcast.61), kind=kOutput, calls=%fused_computation.18 | convolution fusion | flops 808845312 | bytes 14690304 | tf_op jit(solution)/shard_map/sjt,std->sjd/dot_general | solution.py:108
  130.0 2.6 copy-done.1
  132.6 6.6 %fusion.2 = bf16[768,2048]{1,0:T(8,128)(2,1)} fusion(bf16[768,1536]{1,0:T(8,128)(2,1)S(1)} %bitcast.59, bf16[1536,2048]{1,0:T(8,128)(2,1)S(1)} %bitcast.57, bf16[1536]{0:T(1024)(128)(2,1)S(1)} %convert_element_type.78), kind=kOutput, calls=%fused_computation.22 | convolution fusion | flops 4836556800 | bytes 11799552 | tf_op jit(solution)/shard_map/dot_general | solution.py:153
  139.3 8.7 %multiply_reduce_fusion = f32[1536]{0:T(1024)S(1)} fusion(bf16[1536,2048]{1,0:T(8,128)(2,1)} %bitcast.58, bf16[1,768,2048]{2,1,0:T(8,128)(2,1)} %all-gather.6.cloned.1.call-done, bf16[1,1,1536,768]{2,3,1,0:T(8,128)(2,1)} %copy-done.3), kind=kOutput, calls=%fused_computation.17 | convolution fusion | flops 4835375616 | bytes 11802624 | tf_op jit(solution)/shard_map/dot_general | solution.py:146
  148.0 0.7 all_to_all.8
  148.6 5.9 %all-to-all-start = ((f32[16,1,96]{2,1,0:T(1,128)}), f32[16,1,96]{2,1,0:T(1,128)S(1)}, u32[]{:S(2)}, u32[]{:S(2)}) async-start(f32[16,1,96]{2,1,0:T(1,128)} %all_to_all.8), calls=%async_computation.1 | async-start | bytes 16384 | tf_op jit(solution)/shard_map/all_to_all | solution.py:165
  154.6 4.2 %fusion.16 = (bf16[1,384,2048]{2,1,0:T(8,128)(2,1)S(1)}, bf16[1,384,2048]{2,1,0:T(8,128)(2,1)S(1)}, bf16[1,384,2048]{2,1,0:T(8,128)(2,1)S(1)}) fusion(bf16[1,384,2048]{2,1,0:T(8,128)(2,1)S(1)} %copy-done.4, bf16[384,2048]{1,0:T(8,128)(2,1)} %reduce-scatter.2.cloned.1.call-done, bf16[1,384,2048]{2,1,0:T(8,128)(2,1)} %param.24, ...), kind=kLoop, calls=%fused_computation.34 | loop fusion | flops 15728640 | bytes 11010048 | tf_op jit(solution)/shard_map/stack | solution.py:163
  158.8 2.4 pad_maximum_fusion
  161.2 1.5 collective-permute-start.12
  162.6 1.5 collective-permute-start.13
  164.1 210.3 %conditional.1 = (bf16[3,384,2048]{2,1,0:T(8,128)(2,1)}) conditional(s32[]{:T(128)} %clamp.3, bf16[3,384,2048]{2,1,0:T(8,128)(2,1)} %pad_maximum_fusion, (s32[]{:T(128)}, pred[]{:T(512)}, bf16[3,384,2048]{2,1,0:T(8,128)(2,1)}) %tuple.38, (s32[]{:T(128)}, pred[]{:T(512)}, bf16[3,384,2048]{2,1,0:T(8,128)(2,1)}) %tuple.39, ...), branch_computations={%region_19.20_spmd, %region_20.21_spmd, %region_21.22_spmd, %regio... | conditional | flops 7077901 | bytes 80216312 | solution.py:201
  164.8 4.3 %collective-permute-start.6 = (bf16[3,384,2048]{2,1,0:T(8,128)(2,1)}, bf16[3,384,2048]{2,1,0:T(8,128)(2,1)}, u32[]{:S(2)}, u32[]{:S(2)}) collective-permute-start(bf16[3,384,2048]{2,1,0:T(8,128)(2,1)} %get-tuple-element.78), channel_id=1, source_target_pairs={{4,12},{5,13},{6,14},{7,15},{12,4},{13,5},{14,6},{15,7},{20,28},{2... | collective-permute-start | bytes 14155784 | tf_op jit(solution)/shard_map/cond/branch_5_fun/ppermute | solution.py:184
  170.3 97.0 %collective-permute-done.5 = bf16[3,384,2048]{2,1,0:T(8,128)(2,1)} collective-permute-done((bf16[3,384,2048]{2,1,0:T(8,128)(2,1)}, bf16[3,384,2048]{2,1,0:T(8,128)(2,1)}, u32[]{:S(2)}, u32[]{:S(2)}) %collective-permute-start.5) | collective-permute-done | bytes 4718624 | tf_op jit(solution)/shard_map/cond/branch_5_fun/ppermute | solution.py:184
  267.3 102.0 %collective-permute-done.6 = bf16[3,384,2048]{2,1,0:T(8,128)(2,1)} collective-permute-done((bf16[3,384,2048]{2,1,0:T(8,128)(2,1)}, bf16[3,384,2048]{2,1,0:T(8,128)(2,1)}, u32[]{:S(2)}, u32[]{:S(2)}) %collective-permute-start.6) | collective-permute-done | bytes 4718624 | tf_op jit(solution)/shard_map/cond/branch_5_fun/ppermute | solution.py:184
  369.3 5.1 %select_select_fusion.1 = bf16[3,384,2048]{2,1,0:T(8,128)(2,1)} fusion(bf16[3,384,2048]{2,1,0:T(8,128)(2,1)} %get-tuple-element.78, bf16[3,384,2048]{2,1,0:T(8,128)(2,1)} %collective-permute-done.5, bf16[3,384,2048]{2,1,0:T(8,128)(2,1)} %collective-permute-done.6, pred[]{:T(512)S(6)} %select_n.178, pred[]{:T(512)S(6)} %select_n.176), kind=kLoop, calls=%fused_computation.8 | loop fusion | flops 4718592 | bytes 18874370 | tf_op jit(solution)/shard_map/cond/branch_5_fun/select_n | solution.py:197
  374.4 0.8 select_reduce_fusion
  375.9 4.4 %select_select_fusion.4 = bf16[3,384,2048]{2,1,0:T(8,128)(2,1)S(1)} fusion(bf16[3,384,2048]{2,1,0:T(8,128)(2,1)} %get-tuple-element.126, bf16[3,384,2048]{2,1,0:T(8,128)(2,1)} %collective-permute-done.12, bf16[3,384,2048]{2,1,0:T(8,128)(2,1)} %collective-permute-done.13, pred[]{:T(512)S(6)} %select_n.246, pred[]{:T(512)S(6)} %select_n.244), kind=kLoop, calls=%fused_computation.16 | loop fusion | flops 4718592 | bytes 18874370 | tf_op jit(solution)/shard_map/select_n | solution.py:203
  380.3 2.4 fusion.24
  (59 shorter events, 4.9 us)
Async XLA Ops:
  7.2 117.7 %all-gather.4.cloned.1.call-start = ((), (), s32[]{:S(2)}) async-start(), calls=%async_computation.2 | async-start | bytes 8912896 | tf_op jit(solution)/shard_map/all_gather | solution.py:98
  7.9 131.4 %all-gather.6.cloned.1.call-start = ((), (), s32[]{:S(2)}) async-start(), calls=%async_computation.4 | async-start | bytes 4718592 | tf_op jit(solution)/shard_map/all_gather | solution.py:55
  8.6 145.9 %reduce-scatter.2.cloned.1.call-start = ((), (), s32[]{:S(2)}) async-start(), calls=%async_computation.3 | async-start | bytes 4718592 | tf_op jit(solution)/shard_map/reduce_scatter | solution.py:157
  12.9 117.1 %copy-start.3 = (bf16[1,1,1536,768]{2,3,1,0:T(8,128)(2,1)}, bf16[1,1,1536,768]{2,3,1,0:T(8,128)(2,1)S(1)}, u32[]{:S(2)}) copy-start(bf16[1,1,1536,768]{2,3,1,0:T(8,128)(2,1)S(1)} %copy.41) | copy-start | bytes 7077892
  13.4 7.3 %copy-start.6 = (s32[128,8]{0,1:T(8,128)S(1)}, s32[128,8]{0,1:T(8,128)}, u32[]{:S(2)}) copy-start(s32[128,8]{0,1:T(8,128)} %param.20) | copy-start | bytes 12292
  13.5 7.3 %copy-start.5 = (f32[128,8]{0,1:T(8,128)S(1)}, f32[128,8]{0,1:T(8,128)}, u32[]{:S(2)}) copy-start(f32[128,8]{0,1:T(8,128)} %param.21) | copy-start | bytes 12292
  13.5 44.4 %copy-start = (s32[16]{0:T(128)S(1)}, s32[16]{0:T(128)}, u32[]{:S(2)}) copy-start(s32[16]{0:T(128)} %param.26) | copy-start | bytes 196
  13.5 49.6 %copy-start.7 = (s32[8]{0:T(128)S(1)}, s32[8]{0:T(128)}, u32[]{:S(2)}) copy-start(s32[8]{0:T(128)} %constant.72.clone) | copy-start | bytes 100
  13.5 50.2 %copy-start.10 = (s32[8]{0:T(128)S(1)}, s32[8]{0:T(128)}, u32[]{:S(2)}) copy-start(s32[8]{0:T(128)} %constant.138) | copy-start | bytes 100
  13.5 51.5 %copy-start.8 = (s32[8]{0:T(128)S(1)}, s32[8]{0:T(128)}, u32[]{:S(2)}) copy-start(s32[8]{0:T(128)} %constant.128.clone) | copy-start | bytes 100
  13.5 52.2 %copy-start.9 = (s32[8]{0:T(128)S(1)}, s32[8]{0:T(128)}, u32[]{:S(2)}) copy-start(s32[8]{0:T(128)} %constant.143) | copy-start | bytes 100
  130.0 2.7 copy-start.1
  139.2 15.4 %copy-start.2 = (bf16[1,384,2048]{2,1,0:T(8,128)(2,1)S(1)}, bf16[1,384,2048]{2,1,0:T(8,128)(2,1)}, u32[]{:S(2)}) copy-start(bf16[1,384,2048]{2,1,0:T(8,128)(2,1)} %param.23) | copy-start | bytes 4718596
  139.2 15.4 %copy-start.4 = (bf16[1,384,2048]{2,1,0:T(8,128)(2,1)S(1)}, bf16[1,384,2048]{2,1,0:T(8,128)(2,1)}, u32[]{:S(2)}) copy-start(bf16[1,384,2048]{2,1,0:T(8,128)(2,1)} %param.25) | copy-start | bytes 4718596
  148.6 12.5 %all-to-all-start = ((f32[16,1,96]{2,1,0:T(1,128)}), f32[16,1,96]{2,1,0:T(1,128)S(1)}, u32[]{:S(2)}, u32[]{:S(2)}) async-start(f32[16,1,96]{2,1,0:T(1,128)} %all_to_all.8), calls=%async_computation.1 | async-start | bytes 16384 | tf_op jit(solution)/shard_map/all_to_all | solution.py:165
  161.2 214.7 %collective-permute-start.12 = (bf16[3,384,2048]{2,1,0:T(8,128)(2,1)}, bf16[3,384,2048]{2,1,0:T(8,128)(2,1)}, u32[]{:S(2)}, u32[]{:S(2)}) collective-permute-start(bf16[3,384,2048]{2,1,0:T(8,128)(2,1)} %pad_maximum_fusion), channel_id=1, source_target_pairs={{0,1},{1,0},{2,3},{3,2},{4,5},{5,4},{6,7},{7,6},{8,9},{9,8},{10,11... | collective-permute-start | bytes 14155784 | tf_op jit(solution)/shard_map/ppermute | solution.py:184
  162.6 213.2 %collective-permute-start.13 = (bf16[3,384,2048]{2,1,0:T(8,128)(2,1)}, bf16[3,384,2048]{2,1,0:T(8,128)(2,1)}, u32[]{:S(2)}, u32[]{:S(2)}) collective-permute-start(bf16[3,384,2048]{2,1,0:T(8,128)(2,1)} %pad_maximum_fusion), channel_id=1, source_target_pairs={{0,2},{1,3},{2,0},{3,1},{4,6},{5,7},{6,4},{7,5},{8,10},{9,11},{10,... | collective-permute-start | bytes 14155784 | tf_op jit(solution)/shard_map/ppermute | solution.py:184
  164.1 103.1 %collective-permute-start.5 = (bf16[3,384,2048]{2,1,0:T(8,128)(2,1)}, bf16[3,384,2048]{2,1,0:T(8,128)(2,1)}, u32[]{:S(2)}, u32[]{:S(2)}) collective-permute-start(bf16[3,384,2048]{2,1,0:T(8,128)(2,1)} %get-tuple-element.78), channel_id=1, source_target_pairs={{0,4},{1,5},{2,6},{3,7},{4,0},{5,1},{6,2},{7,3},{8,12},{9,13},{10,... | collective-permute-start | bytes 14155784 | tf_op jit(solution)/shard_map/cond/branch_5_fun/ppermute | solution.py:184
  164.8 204.5 %collective-permute-start.6 = (bf16[3,384,2048]{2,1,0:T(8,128)(2,1)}, bf16[3,384,2048]{2,1,0:T(8,128)(2,1)}, u32[]{:S(2)}, u32[]{:S(2)}) collective-permute-start(bf16[3,384,2048]{2,1,0:T(8,128)(2,1)} %get-tuple-element.78), channel_id=1, source_target_pairs={{4,12},{5,13},{6,14},{7,15},{12,4},{13,5},{14,6},{15,7},{20,28},{2... | collective-permute-start | bytes 14155784 | tf_op jit(solution)/shard_map/cond/branch_5_fun/ppermute | solution.py:184
Sparse Core Ops, SparseCore 0:
  10.8 113.9 all-gather.3
  126.4 11.7 all-gather.5
  140.4 12.0 reduce-scatter.1
